TPU v7x, 768 devices: a whole 4x8x12 slice. The times are simulated.
768 devices in a mesh: dp: 32 (over y, x), fsdp: 24 (over z, core).
Axes of the slice: x: 4, y: 8, z: 12, core: 2. Of those that a mesh axis runs over, the one named last changes fastest.
Arguments:
- waveform: bfloat16 [24576, 50], P(('dp', 'fsdp')), may hold values from -6 to 6
- destination: int32 [24576, 1], P(('dp', 'fsdp')), may hold values from 0 to 31; in each aligned block of 32 rows (0 to 31, 32 to 63, ...) at most 2 rows name the same one
- lengths: int32 [24576], P(('dp', 'fsdp')), may hold values from 20 to 50
- conv0_weight: bfloat16 [10, 512], replicated, may hold values from -2 to 2
- conv1_weight: bfloat16 [1536, 512], replicated, may hold values from -0.15625 to 0.15625
- norm_gain: float32 [3, 512], replicated, may hold values from 0.1 to 1.9
- norm_bias: float32 [3, 512], replicated, may hold values from -3 to 3
- proj_weight: bfloat16 [512, 1920], P(None, 'fsdp'), may hold values from -0.25 to 0.25
- proj_bias: bfloat16 [1920], P('fsdp'), may hold values from -3 to 3
- cotangent: bfloat16 [49152, 4, 1920], P(('dp', 'fsdp')), may hold values from -0.078125 to 0.078125
Outputs:
- features: bfloat16 [49152, 4, 1920], P(('dp', 'fsdp'))
- grad_proj_weight: bfloat16 [512, 1920], P(None, 'fsdp')
- grad_proj_bias: bfloat16 [1920], P('fsdp')
Inputs may be any that keep to these rules, and one draw needn't show every extreme that they name: On each device no destination is named by more than 2 of its rows, and on some devices one destination is named by exactly 2 rows.
All inputs are finite; a program needn't handle non-finite values.
Results may differ from a plain program's by a relative error of at most 0.0064.
Values may be sent and summed in bfloat16 or wider, within the bound.
No kernel may reach another device: no remote copies, remote signals or barrier semaphores. Data moves between devices by JAX's collectives and lax.ppermute only.
A program may use at most 64 MiB of HBM per device.

v0:
```python
import jax
import jax.numpy as jnp
from jax import lax
from jax.sharding import PartitionSpec as P


def layer_norm(values, gain_vec, bias_vec):
    avg_value = jnp.mean(values, axis=-1, keepdims=True)
    centred = values - avg_value
    variance = jnp.mean(centred * centred, axis=-1, keepdims=True)
    return centred * lax.rsqrt(variance + 1e-05) * gain_vec + bias_vec


def encode(wave_rows, conv0_weight, conv1_weight, norm_gain, norm_bias):
    row_count = wave_rows.shape[0]
    frame_count = (wave_rows.shape[1] - 10) // 10
    sample_blocks = wave_rows.reshape(row_count, 2 * frame_count + 2, 5)
    sample_pairs = jnp.concatenate([sample_blocks[:, :-1], sample_blocks[:, 1:]], axis=2).reshape(
        -1, 10
    )
    first_conv = jnp.dot(sample_pairs, conv0_weight, preferred_element_type=jnp.float32)
    first_conv = jax.nn.gelu(
        layer_norm(first_conv, norm_gain[0], norm_bias[0]), approximate=False
    ).astype(jnp.bfloat16)
    first_conv = first_conv.reshape(row_count, 2 * frame_count + 1, -1)
    conv_taps = jnp.concatenate(
        [
            first_conv[:, 0 : 2 * frame_count : 2],
            first_conv[:, 1 : 2 * frame_count + 1 : 2],
            first_conv[:, 2 : 2 * frame_count + 2 : 2],
        ],
        axis=2,
    )
    second_conv = jnp.dot(
        conv_taps.reshape(row_count * frame_count, -1),
        conv1_weight,
        preferred_element_type=jnp.float32,
    )
    return jax.nn.gelu(
        layer_norm(second_conv, norm_gain[1], norm_bias[1]), approximate=False
    ).astype(jnp.bfloat16)


def local(
    waveform,
    destination,
    lengths,
    conv0_weight,
    conv1_weight,
    norm_gain,
    norm_bias,
    proj_weight,
    proj_bias,
    cotangent,
):
    dp_size = lax.axis_size("dp")
    row_count = waveform.shape[0]
    slot_count = cotangent.shape[0]
    frame_count = cotangent.shape[1]
    slot_cap = slot_count // dp_size
    weights, biases = (
        lax.all_gather(proj_weight, "fsdp", axis=1, tiled=True),
        lax.all_gather(proj_bias, "fsdp", axis=0, tiled=True),
    )
    targets = destination[:, 0]
    row_order = jnp.arange(row_count, dtype=jnp.int32)
    same_dest = targets[:, None] == targets[None, :]
    earlier_rows = row_order[None, :] < row_order[:, None]
    row_rank = jnp.sum((same_dest & earlier_rows).astype(jnp.int32), axis=1)
    position = targets * slot_cap + row_rank
    placing = position[None, :] == jnp.arange(slot_count, dtype=jnp.int32)[:, None]
    slot_length = jnp.sum(jnp.where(placing, lengths[None, :], 0), axis=1)
    placing_matrix = placing.astype(jnp.bfloat16)
    slot_wave = jnp.dot(placing_matrix, waveform, preferred_element_type=jnp.float32).astype(
        jnp.bfloat16
    )
    got_wave, got_length = (
        lax.all_to_all(
            slot_wave.reshape(dp_size, slot_cap, -1), "dp", split_axis=0, concat_axis=0, tiled=True
        ),
        lax.all_to_all(
            slot_length.reshape(dp_size, slot_cap), "dp", split_axis=0, concat_axis=0, tiled=True
        ),
    )
    hidden = encode(
        got_wave.reshape(slot_count, -1), conv0_weight, conv1_weight, norm_gain, norm_bias
    )
    got_length = got_length.reshape(slot_count)
    normed = layer_norm(hidden.astype(jnp.float32), norm_gain[2], norm_bias[2]).astype(jnp.bfloat16)
    frame_ids = jnp.arange(frame_count, dtype=jnp.int32)
    valid = (10 * frame_ids[None, :] + 20 <= got_length[:, None]).reshape(-1, 1)
    frame_mask = valid.astype(jnp.float32)
    projected = jnp.dot(normed, weights, preferred_element_type=jnp.float32) + biases.astype(
        jnp.float32
    )
    features = (projected * frame_mask).astype(jnp.bfloat16).reshape(slot_count, frame_count, -1)
    cot_rows = cotangent.reshape(slot_count * frame_count, -1)
    grad_out = jnp.where(valid, cot_rows, jnp.zeros_like(cot_rows))
    weight_term = lax.dot_general(
        normed, grad_out, (((0,), (0,)), ((), ())), preferred_element_type=jnp.float32
    )
    bias_term = jnp.sum(grad_out, axis=0, dtype=jnp.float32)
    part_weight, part_bias = (
        lax.psum_scatter(weight_term, "fsdp", scatter_dimension=1, tiled=True),
        lax.psum_scatter(bias_term, "fsdp", scatter_dimension=0, tiled=True),
    )
    grad_weight, grad_bias = lax.psum((part_weight, part_bias), "dp")
    return (features, grad_weight.astype(jnp.bfloat16), grad_bias.astype(jnp.bfloat16))


def solution(mesh):
    in_specs = (
        P(("dp", "fsdp"), None),
        P(("dp", "fsdp"), None),
        P(("dp", "fsdp")),
        P(),
        P(),
        P(),
        P(),
        P(None, "fsdp"),
        P("fsdp"),
        P(("dp", "fsdp"), None, None),
    )
    out_specs = (P(("dp", "fsdp"), None, None), P(None, "fsdp"), P("fsdp"))
    return jax.shard_map(local, mesh=mesh, in_specs=in_specs, out_specs=out_specs, check_vma=False)
```

profile of v0, /device:TPU:32, one launch (start us, length us, event | category | flops | bytes accessed | tf_op | source)
XLA Modules:
  0.0 332.7 jit_solution(6643730137694367772)
XLA Ops:
  7.2 1.0 convert_reduce_fusion.2
  8.1 0.7 multiply_add_fusion.3
  8.8 0.7 select_reduce_fusion
  9.6 0.7 all_to_all.10
  10.3 12.7 %all-to-all-start.1 = ((s32[32,1,2]{2,1,0:T(1,128)}), s32[32,1,2]{2,1,0:T(1,128)S(1)}, u32[]{:S(2)}, u32[]{:S(2)}) async-start(s32[32,1,2]{2,1,0:T(1,128)} %bitcast.9), calls=%async_computation.1 | async-start | bytes 32768 | tf_op jit(solution)/shard_map/all_to_all | solution.py:81
  23.0 0.7 all-gather.2.cloned.1.call-update
  23.7 0.9 convolution_convert_fusion
  24.6 0.8 fusion.39
  25.4 0.8 fusion.40
  26.2 0.7 copy.20
  26.9 1.7 reshape.120
  28.6 9.8 %all-to-all-start = ((bf16[32,2,50]{2,1,0:T(2,128)(2,1)}), bf16[32,2,50]{2,1,0:T(2,128)(2,1)S(1)}, u32[]{:S(2)}, u32[]{:S(2)}) async-start(bf16[32,2,50]{2,1,0:T(2,128)(2,1)} %bitcast.1), calls=%async_computation | async-start | bytes 32768 | tf_op jit(solution)/shard_map/all_to_all | solution.py:78
  38.5 0.0 reduce-scatter.2.cloned.1.call-start
  38.5 0.5 broadcast.120
  39.0 0.7 reduce.4
  39.7 0.1 le.28
  39.8 0.1 broadcast_compare_fusion
  39.9 0.1 le.31
  40.0 3.1 all-to-all-done
  43.2 0.2 reshape_reshape.3
  43.4 0.1 fusion.38
  43.5 0.2 pad_maximum_fusion.1
  43.7 0.1 reshape.126
  43.8 0.3 copy-done.2
  44.1 0.4 fusion.42
  44.5 0.3 multiply_reduce_fusion
  44.8 3.3 fusion.4
  48.1 1.2 reshape.117
  49.3 6.0 %slice.37 = bf16[64,4,512]{2,1,0:T(4,128)(2,1)} slice(bf16[64,9,512]{2,1,0:T(8,128)(2,1)} %reshape.117), slice={[0:64:1], [0:8:2], [0:512:1]} | slice | bytes 524288 | tf_op jit(solution)/shard_map/slice | solution.py:28
  55.3 6.0 %slice.38 = bf16[64,4,512]{2,1,0:T(4,128)(2,1)} slice(bf16[64,9,512]{2,1,0:T(8,128)(2,1)} %reshape.117), slice={[0:64:1], [1:9:2], [0:512:1]} | slice | bytes 524288 | tf_op jit(solution)/shard_map/slice | solution.py:29
  61.3 6.1 %slice.39 = bf16[64,4,512]{2,1,0:T(4,128)(2,1)} slice(bf16[64,9,512]{2,1,0:T(8,128)(2,1)} %reshape.117), slice={[0:64:1], [2:9:2], [0:512:1]} | slice | bytes 524288 | tf_op jit(solution)/shard_map/slice | solution.py:30
  67.3 1.5 pad_maximum_fusion
  68.8 1.1 reshape.118
  69.9 1.8 fusion.43
  71.7 0.2 multiply_reduce_fusion.1
  71.9 1.4 convert_reduce_fusion.1
  73.3 0.2 fusion.17
  73.5 2.8 fusion.12
  76.3 1.4 fusion.41
  78.4 0.2 dynamic-update-slice
  78.6 42.0 %all-reduce = bf16[1920]{0:T(1024)(128)(2,1)S(1)} all-reduce(bf16[1920]{0:T(1024)(128)(2,1)S(1)} %dynamic-update-slice), channel_id=1, replica_groups=mesh['dp'=32,'fsdp'=24] {'fsdp'}, use_global_device_ids=true, to_apply=%add | all-reduce | flops 1920 | bytes 7680
  121.3 0.6 convert_reduce_fusion
  121.9 35.6 %all-reduce.1 = f32[1920]{0:T(1024)S(1)} all-reduce(f32[1920]{0:T(1024)S(1)} %convert_reduce_fusion), channel_id=3, replica_groups=mesh['dp'=32,'fsdp'=24] {'fsdp'}, use_global_device_ids=true, to_apply=%region_11.12.clone | all-reduce | flops 1920 | bytes 15360
  157.5 0.1 dynamic-slice.2
  157.6 2.4 fusion.1
  159.9 1.2 reshape.119
  161.1 21.5 %reduce-scatter.2.cloned.1.call-done = f32[512,80]{0,1:T(8,128)} async-done(((f32[512,1920]{0,1:T(8,128)}), f32[512,80]{0,1:T(8,128)}) %reduce-scatter.2.cloned.1.call-update) | async-done | bytes 163856 | tf_op jit(solution)/shard_map/reduce_scatter | solution.py:104
  182.6 143.3 %all-reduce.4 = (bf16[512,80]{0,1:T(8,128)(2,1)}, bf16[80]{0:T(256)(128)(2,1)}) all-reduce(f32[512,80]{0,1:T(8,128)} %reduce-scatter.2.cloned.1.call-done, f32[80]{0:T(128)S(1)} %dynamic-slice.2), channel_id=1, replica_groups=mesh['dp'=32,'fsdp'=24] {'dp'}, use_global_device_ids=true, to_apply=%region_9.10 | all-reduce | flops 41040 | bytes 246240 | tf_op jit(solution)/shard_map/psum | solution.py:107
  (21 shorter events, 0.1 us)
Async XLA Ops:
  7.2 62.7 %copy-start = (bf16[1536,512]{1,0:T(8,128)(2,1)S(1)}, bf16[1536,512]{1,0:T(8,128)(2,1)}, u32[]{:S(2)}) copy-start(bf16[1536,512]{1,0:T(8,128)(2,1)} %param.14) | copy-start | bytes 4718596
  10.3 18.4 %all-to-all-start.1 = ((s32[32,1,2]{2,1,0:T(1,128)}), s32[32,1,2]{2,1,0:T(1,128)S(1)}, u32[]{:S(2)}, u32[]{:S(2)}) async-start(s32[32,1,2]{2,1,0:T(1,128)} %bitcast.9), calls=%async_computation.1 | async-start | bytes 32768 | tf_op jit(solution)/shard_map/all_to_all | solution.py:81
  23.0 134.6 %all-gather.2.cloned.1.call-start = ((), (), s32[]{:S(2)}) async-start(), calls=%async_computation.3 | async-start | bytes 2048000 | tf_op jit(solution)/shard_map/all_gather | solution.py:62
  28.6 14.5 %all-to-all-start = ((bf16[32,2,50]{2,1,0:T(2,128)(2,1)}), bf16[32,2,50]{2,1,0:T(2,128)(2,1)S(1)}, u32[]{:S(2)}, u32[]{:S(2)}) async-start(bf16[32,2,50]{2,1,0:T(2,128)(2,1)} %bitcast.1), calls=%async_computation | async-start | bytes 32768 | tf_op jit(solution)/shard_map/all_to_all | solution.py:78
  38.5 144.2 %reduce-scatter.2.cloned.1.call-start = ((), (), s32[]{:S(2)}) async-start(), calls=%async_computation.4 | async-start | bytes 4096000 | tf_op jit(solution)/shard_map/reduce_scatter | solution.py:104
  43.4 0.7 copy-start.2
  76.3 2.1 copy-start.3
  76.3 45.0 %copy-start.1 = (bf16[64,4,1920]{2,1,0:T(4,128)(2,1)S(1)}, bf16[64,4,1920]{2,1,0:T(4,128)(2,1)}, u32[]{:S(2)}) copy-start(bf16[64,4,1920]{2,1,0:T(4,128)(2,1)} %param.19) | copy-start | bytes 2949124
Sparse Core Ops, SparseCore 0:
  26.2 63.5 all-gather.1
  92.9 89.6 reduce-scatter.1
where the time goes:
time: 334 us; the launch traced here: 333 us
  blocking collectives  221 us (66%)
  local copies, waits for them, and re-layouts  29.4 us (9%)
  waiting for transfers between devices  25.4 us (8%)
  starting transfers between devices  22.6 us (7%)
  between operations  15.6 us (5%)
  other arithmetic  10.8 us (3%)
  matrix products  8.19 us (2%)
    psum x1, blocking collectives, local(): grad_weight, grad_bias = lax.psum((part_weight, part_bias), 'dp')  143 us
    unnamed x2, blocking collectives  77.5 us
    reduce_scatter x1, waiting for transfers between devices, local(): lax.psum_scatter(weight_term, 'fsdp', scatter_dimension=1, tiled=True)  21.5 us
    all_to_all x1, starting transfers between devices, local(): lax.all_to_all(slot_length.reshape(dp_size, slot_cap), 'dp', split_axis=0...  12.7 us
    all_to_all x1, starting transfers between devices, local(): lax.all_to_all(slot_wave.reshape(dp_size, slot_cap, -1), 'dp', split_axis...  9.8 us
  transfers between devices with their start and end apart: 4, of which 2 were waited for; matrix products, arithmetic and copies ran while one was open for 14% of the time, Pallas kernels for 0%

commit v1 on v0

v1 whole, which is shorter than its diff:
```python
import jax
import jax.numpy as jnp
from jax import lax
from jax.sharding import PartitionSpec as P


def layer_norm(values, gain_vec, bias_vec):
    avg_value = jnp.mean(values, axis=-1, keepdims=True)
    centred = values - avg_value
    variance = jnp.mean(centred * centred, axis=-1, keepdims=True)
    return centred * lax.rsqrt(variance + 1e-05) * gain_vec + bias_vec


def encode(wave_rows, frame_count, conv0_weight, conv1_weight, norm_gain, norm_bias):
    row_count = wave_rows.shape[0]
    taps = 3
    span = 10 * frame_count
    sample_pairs = jnp.concatenate(
        [
            wave_rows[:, 5 * k : 5 * k + span].reshape(row_count * frame_count, 10)
            for k in range(taps)
        ],
        axis=0,
    )
    first_conv = jnp.dot(sample_pairs, conv0_weight, preferred_element_type=jnp.float32)
    first_conv = jax.nn.gelu(
        layer_norm(first_conv, norm_gain[0], norm_bias[0]), approximate=False
    ).astype(jnp.bfloat16)
    channels = conv0_weight.shape[1]
    first_conv = first_conv.reshape(taps, row_count * frame_count, channels)
    second_conv = jnp.einsum(
        "krc,kcd->rd",
        first_conv,
        conv1_weight.reshape(taps, channels, -1),
        preferred_element_type=jnp.float32,
    )
    return jax.nn.gelu(
        layer_norm(second_conv, norm_gain[1], norm_bias[1]), approximate=False
    ).astype(jnp.bfloat16)


def local(
    waveform,
    destination,
    lengths,
    conv0_weight,
    conv1_weight,
    norm_gain,
    norm_bias,
    proj_weight,
    proj_bias,
    cotangent,
):
    dp_size = lax.axis_size("dp")
    row_count, samples = waveform.shape
    slot_count = cotangent.shape[0]
    frame_count = cotangent.shape[1]
    d_conv = proj_weight.shape[0]
    slot_cap = slot_count // dp_size
    weight_and_bias = lax.all_gather(
        jnp.concatenate([proj_weight, proj_bias[None, :]], axis=0), "fsdp", axis=1, tiled=True
    )
    weights, biases = weight_and_bias[:d_conv], weight_and_bias[d_conv]
    targets = destination[:, 0]
    row_order = jnp.arange(row_count, dtype=jnp.int32)
    same_dest = targets[:, None] == targets[None, :]
    earlier_rows = row_order[None, :] < row_order[:, None]
    row_rank = jnp.sum((same_dest & earlier_rows).astype(jnp.int32), axis=1)
    position = targets * slot_cap + row_rank
    placing = position[None, :] == jnp.arange(slot_count, dtype=jnp.int32)[:, None]
    rows_ext = jnp.concatenate([waveform, lengths.astype(jnp.bfloat16)[:, None]], axis=1)
    slot_rows = jnp.dot(
        placing.astype(jnp.bfloat16), rows_ext, preferred_element_type=jnp.float32
    ).astype(jnp.bfloat16)
    got = lax.all_to_all(
        slot_rows.reshape(dp_size, slot_cap, -1), "dp", split_axis=0, concat_axis=0, tiled=True
    ).reshape(slot_count, -1)
    got_wave = got[:, :samples]
    got_length = got[:, samples].astype(jnp.float32)
    hidden = encode(got_wave, frame_count, conv0_weight, conv1_weight, norm_gain, norm_bias)
    normed = layer_norm(hidden.astype(jnp.float32), norm_gain[2], norm_bias[2]).astype(jnp.bfloat16)
    frame_ids = jnp.arange(frame_count, dtype=jnp.float32)
    valid = (10 * frame_ids[None, :] + 20 <= got_length[:, None]).reshape(-1, 1)
    frame_mask = valid.astype(jnp.float32)
    projected = jnp.dot(normed, weights, preferred_element_type=jnp.float32) + biases.astype(
        jnp.float32
    )
    features = (projected * frame_mask).astype(jnp.bfloat16).reshape(slot_count, frame_count, -1)
    cot_rows = cotangent.reshape(slot_count * frame_count, -1)
    grad_out = jnp.where(valid, cot_rows, jnp.zeros_like(cot_rows))
    normed_ext = jnp.concatenate([normed, jnp.ones((normed.shape[0], 1), normed.dtype)], axis=1)
    grad_term = lax.dot_general(
        normed_ext, grad_out, (((0,), (0,)), ((), ())), preferred_element_type=jnp.float32
    )
    part = lax.psum_scatter(grad_term, "fsdp", scatter_dimension=1, tiled=True)
    total = lax.reduce_precision(lax.psum(part, "dp"), exponent_bits=8, mantissa_bits=7)
    grad_weight, grad_bias = total[:d_conv], total[d_conv]
    return (features, grad_weight.astype(jnp.bfloat16), grad_bias.astype(jnp.bfloat16))


def solution(mesh):
    in_specs = (
        P(("dp", "fsdp"), None),
        P(("dp", "fsdp"), None),
        P(("dp", "fsdp")),
        P(),
        P(),
        P(),
        P(),
        P(None, "fsdp"),
        P("fsdp"),
        P(("dp", "fsdp"), None, None),
    )
    out_specs = (P(("dp", "fsdp"), None, None), P(None, "fsdp"), P("fsdp"))
    return jax.shard_map(local, mesh=mesh, in_specs=in_specs, out_specs=out_specs, check_vma=False)
```

time: 334 us -> 363 us (1.087)
  the two profiles are of different devices: /device:TPU:32 before, /device:TPU:2 now
where the time goes in v1:
time: 363 us; the launch traced here: 362 us
  waiting for transfers between devices  306 us (84%)
  between operations  13.9 us (4%)
  other arithmetic  13.2 us (4%)
  starting transfers between devices  13.1 us (4%)
  local copies, waits for them, and re-layouts  8.86 us (2%)
  matrix products  7.64 us (2%)
    psum x1, waiting for transfers between devices, local(): lax.psum(part, 'dp')  164 us
    reduce_scatter x1, waiting for transfers between devices, local(): part = lax.psum_scatter(grad_term, 'fsdp', scatter_dimension=1, tiled=True)  93.2 us
    all_gather x1, waiting for transfers between devices, local(): lax.all_gather(jnp.concatenate([proj_weight, proj_bias[None, :]], axis=0)...  46.5 us
    all_to_all x1, starting transfers between devices, local(): lax.all_to_all(slot_rows.reshape(dp_size, slot_cap, -1), 'dp', split_axis...  13 us
  transfers between devices with their start and end apart: 4, of which 4 were waited for; matrix products, arithmetic and copies ran while one was open for 6% of the time, Pallas kernels for 0%

profile of v1, /device:TPU:2, one launch (start us, length us, event | category | flops | bytes accessed | tf_op | source)
XLA Modules:
  0.0 362.3 jit_solution(312755797004641927)
XLA Ops:
  7.2 0.0 copy-start
  7.2 0.8 convert_bitcast_fusion
  8.0 0.1 copy.27
  8.1 0.9 convert_reduce_fusion.3
  9.0 0.7 multiply_add_fusion.3
  9.7 1.0 convolution_convert_fusion
  10.6 0.7 copy.28
  11.3 13.0 %all-to-all-start = ((bf16[32,2,51]{2,1,0:T(2,128)(2,1)}), bf16[32,2,51]{2,1,0:T(2,128)(2,1)S(1)}, u32[]{:S(2)}, u32[]{:S(2)}) async-start(bf16[32,2,51]{2,1,0:T(2,128)(2,1)} %bitcast.2), calls=%async_computation | async-start | bytes 32768 | tf_op jit(solution)/shard_map/all_to_all | solution.py:75
  24.3 0.0 all-gather.2.cloned.1.call-start
  24.4 0.8 copy.32
  25.1 1.5 pad_maximum_fusion
  26.7 0.0 all-gather.2.cloned.1.call-update
  26.7 0.0 reduce-scatter.2.cloned.1.call-start
  26.8 0.8 fusion.51
  27.6 0.8 fusion.52
  28.4 2.4 reshape.120
  30.9 2.1 all-to-all-done
  32.9 0.1 fusion.50
  33.0 0.2 convert_reduce_fusion.2
  33.2 0.1 reshape.114
  33.3 0.1 copy.29
  33.4 0.1 reshape.115
  33.5 0.1 copy.30
  33.6 0.1 reshape.116
  33.7 0.1 copy.31
  33.8 0.5 fusion.53
  34.3 0.3 multiply_reduce_fusion
  34.6 0.1 broadcast_compare_fusion
  34.7 0.1 le.34
  34.8 4.5 %fusion.5 = bf16[768,512]{1,0:T(8,128)(2,1)S(1)} fusion(f32[768,512]{1,0:T(8,128)S(1)} %get-tuple-element.15, f32[512]{0:T(512)S(1)} %bitcast.30, f32[512]{0:T(512)S(1)} %bitcast.29, f32[768]{0:T(1024)S(1)} %add_rsqrt_fusion, f32[768]{0:T(1024)S(1)} %broadcast_multiply_fusion), kind=kLoop, calls=%fused_computation.7 | loop fusion | flops 27131904 | bytes 2369536 | tf_op jit(solution)/shard_map/convert_element_type | solution.py:28
  39.3 0.6 fusion.54
  40.0 0.2 multiply_reduce_fusion.1
  40.2 1.4 convert_reduce_fusion.1
  41.6 0.2 fusion.18
  41.8 0.2 fusion.21
  42.0 3.3 fusion.13
  45.3 0.0 reduce-scatter.2.cloned.1.call-update
  45.3 0.0 all-reduce.3.cloned.1.call-start
  45.4 46.5 %all-gather.2.cloned.1.call-done = bf16[513,1920]{0,1:T(8,128)(2,1)} async-done(((bf16[513,80]{0,1:T(8,128)(2,1)}), bf16[513,1920]{0,1:T(8,128)(2,1)}) %all-gather.2.cloned.1.call-update) | async-done | bytes 1969936 | tf_op jit(solution)/shard_map/all_gather | solution.py:60
  91.9 1.2 convert_reduce_fusion
  93.1 93.2 %reduce-scatter.2.cloned.1.call-done = f32[513,80]{0,1:T(8,128)} async-done(((f32[513,1920]{0,1:T(8,128)}), f32[513,80]{0,1:T(8,128)}) %reduce-scatter.2.cloned.1.call-update) | async-done | bytes 164176 | tf_op jit(solution)/shard_map/reduce_scatter | solution.py:95
  186.3 0.0 all-reduce.3.cloned.1.call-update
  186.3 2.3 fusion.1
  188.6 1.2 reshape.119
  189.8 163.8 %all-reduce.3.cloned.1.call-done = f32[513,80]{0,1:T(8,128)} async-done(((f32[513,80]{0,1:T(8,128)}), f32[513,80]{0,1:T(8,128)}) %all-reduce.3.cloned.1.call-update) | async-done | bytes 164176 | tf_op jit(solution)/shard_map/psum | solution.py:96
  353.6 0.9 reduce-precision_convert_fusion
  354.6 0.6 slice.68
  355.2 0.6 slice_reduce_fusion
  (13 shorter events, 0.1 us)
Async XLA Ops:
  7.2 32.1 %copy-start = (bf16[1536,512]{1,0:T(8,128)(2,1)S(1)}, bf16[1536,512]{1,0:T(8,128)(2,1)}, u32[]{:S(2)}) copy-start(bf16[1536,512]{1,0:T(8,128)(2,1)} %param.14) | copy-start | bytes 4718596
  7.2 26.6 %copy-start.2 = (bf16[10,512]{1,0:T(8,128)(2,1)S(1)}, bf16[10,512]{1,0:T(8,128)(2,1)}, u32[]{:S(2)}) copy-start(bf16[10,512]{1,0:T(8,128)(2,1)} %param.13) | copy-start | bytes 30724
  11.3 21.6 %all-to-all-start = ((bf16[32,2,51]{2,1,0:T(2,128)(2,1)}), bf16[32,2,51]{2,1,0:T(2,128)(2,1)S(1)}, u32[]{:S(2)}, u32[]{:S(2)}) async-start(bf16[32,2,51]{2,1,0:T(2,128)(2,1)} %bitcast.2), calls=%async_computation | async-start | bytes 32768 | tf_op jit(solution)/shard_map/all_to_all | solution.py:75
  24.3 67.6 %all-gather.2.cloned.1.call-start = ((), (), s32[]{:S(2)}) async-start(), calls=%async_computation.2 | async-start | bytes 2560000 | tf_op jit(solution)/shard_map/all_gather | solution.py:60
  26.7 159.6 %reduce-scatter.2.cloned.1.call-start = ((), (), s32[]{:S(2)}) async-start(), calls=%async_computation.3 | async-start | bytes 5120000 | tf_op jit(solution)/shard_map/reduce_scatter | solution.py:95
  39.9 2.1 copy-start.1
  45.3 308.3 %all-reduce.3.cloned.1.call-start = ((), (), s32[]{:S(2)}) async-start(), calls=%async_computation.4 | async-start | bytes 409600 | tf_op jit(solution)/shard_map/psum | solution.py:96
Sparse Core Ops, SparseCore 0:
  27.6 64.2 all-gather.1
  95.0 91.2 reduce-scatter.1
  189.8 163.7 all-reduce.2

commit v2 on v1

--- a/solution.py
+++ b/solution.py
@@ -39,7 +39,7 @@
     ).astype(jnp.bfloat16)
 
 
-def local(
+def step(
     waveform,
     destination,
     lengths,
@@ -57,10 +57,16 @@
     frame_count = cotangent.shape[1]
     d_conv = proj_weight.shape[0]
     slot_cap = slot_count // dp_size
-    weight_and_bias = lax.all_gather(
-        jnp.concatenate([proj_weight, proj_bias[None, :]], axis=0), "fsdp", axis=1, tiled=True
+    fsdp_size = lax.axis_size("fsdp")
+    own_block = jnp.concatenate([proj_weight, proj_bias[None, :]], axis=0)
+    blocks = lax.all_to_all(
+        jnp.broadcast_to(own_block[None], (fsdp_size,) + own_block.shape),
+        "fsdp",
+        split_axis=0,
+        concat_axis=0,
+        tiled=True,
     )
-    weights, biases = weight_and_bias[:d_conv], weight_and_bias[d_conv]
+    weights, biases = blocks[:, :d_conv], blocks[:, d_conv].reshape(-1)
     targets = destination[:, 0]
     row_order = jnp.arange(row_count, dtype=jnp.int32)
     same_dest = targets[:, None] == targets[None, :]
@@ -82,9 +88,9 @@
     frame_ids = jnp.arange(frame_count, dtype=jnp.float32)
     valid = (10 * frame_ids[None, :] + 20 <= got_length[:, None]).reshape(-1, 1)
     frame_mask = valid.astype(jnp.float32)
-    projected = jnp.dot(normed, weights, preferred_element_type=jnp.float32) + biases.astype(
-        jnp.float32
-    )
+    projected = jnp.einsum(
+        "rc,jcn->rjn", normed, weights, preferred_element_type=jnp.float32
+    ).reshape(normed.shape[0], -1) + biases.astype(jnp.float32)
     features = (projected * frame_mask).astype(jnp.bfloat16).reshape(slot_count, frame_count, -1)
     cot_rows = cotangent.reshape(slot_count * frame_count, -1)
     grad_out = jnp.where(valid, cot_rows, jnp.zeros_like(cot_rows))
@@ -93,7 +99,11 @@
         normed_ext, grad_out, (((0,), (0,)), ((), ())), preferred_element_type=jnp.float32
     )
     part = lax.psum_scatter(grad_term, "fsdp", scatter_dimension=1, tiled=True)
-    total = lax.reduce_precision(lax.psum(part, "dp"), exponent_bits=8, mantissa_bits=7)
+    total = part
+    bit = 1
+    while bit < dp_size:
+        total = total + lax.ppermute(total, "dp", [(i, i ^ bit) for i in range(dp_size)])
+        bit *= 2
     grad_weight, grad_bias = total[:d_conv], total[d_conv]
     return (features, grad_weight.astype(jnp.bfloat16), grad_bias.astype(jnp.bfloat16))
 
@@ -112,4 +122,4 @@
         P(("dp", "fsdp"), None, None),
     )
     out_specs = (P(("dp", "fsdp"), None, None), P(None, "fsdp"), P("fsdp"))
-    return jax.shard_map(local, mesh=mesh, in_specs=in_specs, out_specs=out_specs, check_vma=False)
+    return jax.shard_map(step, mesh=mesh, in_specs=in_specs, out_specs=out_specs, check_vma=False)

time: 363 us -> 261 us (0.72)
  the two profiles are of different devices: /device:TPU:2 before, /device:TPU:199 now
where the time goes in v2:
time: 261 us
  waiting for transfers between devices  164 us (63%)
  starting transfers between devices  41.5 us (16%)
  local copies, waits for them, and re-layouts  17.5 us (7%)
  other arithmetic  16.4 us (6%)
  between operations  14.3 us (5%)
  matrix products  7.01 us (3%)
    reduce_scatter x1, waiting for transfers between devices, step(): part = lax.psum_scatter(grad_term, 'fsdp', scatter_dimension=1, tiled=True)  135 us
    ppermute x5, waiting for transfers between devices, step(): lax.ppermute(total, 'dp', [(i, i ^ bit) for i in range(dp_size)])  25.1 us
    ppermute x5, starting transfers between devices, step(): lax.ppermute(total, 'dp', [(i, i ^ bit) for i in range(dp_size)])  17.1 us
    all_to_all x1, starting transfers between devices, step(): lax.all_to_all(jnp.broadcast_to(own_block[None], (fsdp_size,) + own_block...  14.8 us
    all_to_all x1, starting transfers between devices, step(): lax.all_to_all(slot_rows.reshape(dp_size, slot_cap, -1), 'dp', split_axis...  9.63 us
  transfers between devices with their start and end apart: 8, of which 7 were waited for; matrix products, arithmetic and copies ran while one was open for 7% of the time, Pallas kernels for 0%

profile of v2, /device:TPU:199, one launch (start us, length us, event | category | flops | bytes accessed | tf_op | source)
XLA Modules:
  0.0 260.6 jit_solution(9260113027152866423)
XLA Ops:
  7.2 0.8 convert_bitcast_fusion
  8.0 0.9 convert_reduce_fusion.3
  8.9 0.7 multiply_add_fusion.3
  9.6 1.0 convolution_convert_fusion
  10.6 0.7 copy.32
  11.3 9.6 %all-to-all-start = ((bf16[32,2,51]{2,1,0:T(2,128)(2,1)}), bf16[32,2,51]{2,1,0:T(2,128)(2,1)S(1)}, u32[]{:S(2)}, u32[]{:S(2)}) async-start(bf16[32,2,51]{2,1,0:T(2,128)(2,1)} %bitcast.2), calls=%async_computation | async-start | bytes 32768 | tf_op jit(solution)/shard_map/all_to_all | solution.py:81
  21.0 0.8 fusion.49
  21.8 0.8 fusion.50
  22.6 1.7 reshape.138
  24.3 3.7 %all-to-all-done = bf16[32,2,51]{2,1,0:T(2,128)(2,1)S(1)} async-done(((bf16[32,2,51]{2,1,0:T(2,128)(2,1)}), bf16[32,2,51]{2,1,0:T(2,128)(2,1)S(1)}, u32[]{:S(2)}, u32[]{:S(2)}) %all-to-all-start) | async-done | bytes 6560 | tf_op jit(solution)/shard_map/all_to_all | solution.py:81
  28.0 0.2 convert_reduce_fusion.2
  28.3 0.7 broadcast_compare_fusion
  29.6 0.5 fusion.51
  30.1 0.3 multiply_reduce_fusion
  30.5 4.5 %fusion.2 = bf16[768,512]{1,0:T(8,128)(2,1)S(1)} fusion(f32[768,512]{1,0:T(8,128)S(1)} %get-tuple-element.17, f32[512]{0:T(512)S(1)} %bitcast.37, f32[512]{0:T(512)S(1)} %bitcast.36, f32[768]{0:T(1024)S(1)} %add_rsqrt_fusion, f32[768]{0:T(1024)S(1)} %broadcast_multiply_fusion), kind=kLoop, calls=%fused_computation.4 | loop fusion | flops 27131904 | bytes 2369536 | tf_op jit(solution)/shard_map/convert_element_type | solution.py:28
  35.0 0.6 fusion.52
  35.6 0.2 multiply_reduce_fusion.1
  35.9 1.4 convert_reduce_fusion.1
  37.3 0.2 fusion.15
  37.5 0.2 fusion.18
  37.7 0.7 copy-done.1
  38.4 3.3 %fusion.10 = f32[513,1920]{0,1:T(8,128)} fusion(bf16[256,1920]{1,0:T(8,128)(2,1)S(1)} %reshape.138, pred[256]{0:T(512)(128)(4,1)S(1)} %le.34, bf16[256,512]{1,0:T(8,128)(2,1)S(1)} %fusion.18), kind=kOutput, calls=%fused_computation.25 | convolution fusion | flops 504791040 | bytes 5185280 | tf_op jit(solution)/shard_map/dot_general | solution.py:98
  41.7 0.6 copy-done.5
  42.6 1.7 broadcast_in_dim.15
  44.3 14.8 %all-to-all-start.1 = ((bf16[24,513,80]{1,2,0:T(8,128)(2,1)}), bf16[24,513,80]{1,2,0:T(8,128)(2,1)}, u32[]{:S(2)}, u32[]{:S(2)}) async-start(bf16[24,513,80]{1,2,0:T(8,128)(2,1)} %broadcast_in_dim.15), calls=%async_computation.1 | async-start | bytes 4915200 | tf_op jit(solution)/shard_map/all_to_all | solution.py:62
  59.0 135.1 %reduce-scatter.2.cloned.1.call-done = f32[513,80]{0,1:T(8,128)} async-done(((f32[513,1920]{0,1:T(8,128)}), f32[513,80]{0,1:T(8,128)}) %reduce-scatter.2.cloned.1.call-update) | async-done | bytes 164176 | tf_op jit(solution)/shard_map/reduce_scatter | solution.py:101
  194.2 2.2 collective-permute-start
  196.4 4.5 %collective-permute-done = f32[513,80]{0,1:T(8,128)S(1)} collective-permute-done((f32[513,80]{0,1:T(8,128)}, f32[513,80]{0,1:T(8,128)S(1)}, u32[]{:S(2)}, u32[]{:S(2)}) %collective-permute-start) | collective-permute-done | bytes 164192 | tf_op jit(solution)/shard_map/ppermute | solution.py:105
  200.9 1.0 add.117
  201.8 3.1 %collective-permute-start.1 = (f32[513,80]{0,1:T(8,128)S(1)}, f32[513,80]{0,1:T(8,128)S(1)}, u32[]{:S(2)}, u32[]{:S(2)}) collective-permute-start(f32[513,80]{0,1:T(8,128)S(1)} %add.117), channel_id=1, source_target_pairs={{0,48},{24,72},{48,0},{72,24},{96,144},{120,168},{144,96},{168,120... | collective-permute-start | bytes 492488 | tf_op jit(solution)/shard_map/ppermute | solution.py:105
  204.9 5.5 %collective-permute-done.1 = f32[513,80]{0,1:T(8,128)S(1)} collective-permute-done((f32[513,80]{0,1:T(8,128)S(1)}, f32[513,80]{0,1:T(8,128)S(1)}, u32[]{:S(2)}, u32[]{:S(2)}) %collective-permute-start.1) | collective-permute-done | bytes 164192 | tf_op jit(solution)/shard_map/ppermute | solution.py:105
  210.4 2.5 collective-permute-start.2
  212.9 1.7 slice.65
  214.6 4.0 %collective-permute-done.2 = f32[513,80]{0,1:T(8,128)S(1)} collective-permute-done((f32[513,80]{0,1:T(8,128)S(1)}, f32[513,80]{0,1:T(8,128)S(1)}, u32[]{:S(2)}, u32[]{:S(2)}) %collective-permute-start.2) | collective-permute-done | bytes 164192 | tf_op jit(solution)/shard_map/ppermute | solution.py:105
  218.6 0.7 add.119
  219.3 5.3 %collective-permute-start.3 = (f32[513,80]{0,1:T(8,128)}, f32[513,80]{0,1:T(8,128)}, u32[]{:S(2)}, u32[]{:S(2)}) collective-permute-start(f32[513,80]{0,1:T(8,128)} %add.119), channel_id=1, source_target_pairs={{0,192},{24,216},{48,240},{72,264},{96,288},{120,312},{144,336},{1... | collective-permute-start | bytes 492488 | tf_op jit(solution)/shard_map/ppermute | solution.py:105
  224.7 1.7 fusion.53
  226.3 1.3 convert_reduce_fusion
  227.6 0.7 reshape.139
  228.3 2.3 copy.37
  230.6 3.4 %reshape.137 = f32[64,4,1920]{2,1,0:T(4,128)S(1)} reshape(f32[256,24,80]{2,1,0:T(8,128)} %copy.37) | data formatting | bytes 3932160 | tf_op jit(solution)/shard_map/reshape | solution.py:93
  234.0 0.6 collective-permute-done.3
  234.6 1.1 add.120
  235.7 4.1 %collective-permute-start.4 = (f32[513,80]{0,1:T(8,128)S(1)}, f32[513,80]{0,1:T(8,128)S(1)}, u32[]{:S(2)}, u32[]{:S(2)}) collective-permute-start(f32[513,80]{0,1:T(8,128)S(1)} %add.120), channel_id=1, source_target_pairs={{0,384},{24,408},{48,432},{72,456},{96,480},{120,504},{144,528},{1... | collective-permute-start | bytes 492488 | tf_op jit(solution)/shard_map/ppermute | solution.py:105
  239.8 2.2 multiply_convert_fusion
  242.0 10.5 %collective-permute-done.4 = f32[513,80]{0,1:T(8,128)S(1)} collective-permute-done((f32[513,80]{0,1:T(8,128)S(1)}, f32[513,80]{0,1:T(8,128)S(1)}, u32[]{:S(2)}, u32[]{:S(2)}) %collective-permute-start.4) | collective-permute-done | bytes 164192 | tf_op jit(solution)/shard_map/ppermute | solution.py:105
  252.5 0.6 slice_reduce_fusion
  253.1 0.6 slice.68
  (33 shorter events, 1.3 us)
Async XLA Ops:
  7.2 27.8 %copy-start = (bf16[1536,512]{1,0:T(8,128)(2,1)S(1)}, bf16[1536,512]{1,0:T(8,128)(2,1)}, u32[]{:S(2)}) copy-start(bf16[1536,512]{1,0:T(8,128)(2,1)} %param.14) | copy-start | bytes 4718596
  7.2 22.5 %copy-start.4 = (bf16[10,512]{1,0:T(8,128)(2,1)S(1)}, bf16[10,512]{1,0:T(8,128)(2,1)}, u32[]{:S(2)}) copy-start(bf16[10,512]{1,0:T(8,128)(2,1)} %param.13) | copy-start | bytes 30724
  11.3 16.7 %all-to-all-start = ((bf16[32,2,51]{2,1,0:T(2,128)(2,1)}), bf16[32,2,51]{2,1,0:T(2,128)(2,1)S(1)}, u32[]{:S(2)}, u32[]{:S(2)}) async-start(bf16[32,2,51]{2,1,0:T(2,128)(2,1)} %bitcast.2), calls=%async_computation | async-start | bytes 32768 | tf_op jit(solution)/shard_map/all_to_all | solution.py:81
  21.0 173.2 %reduce-scatter.2.cloned.1.call-start = ((), (), s32[]{:S(2)}) async-start(), calls=%async_computation.3 | async-start | bytes 5120000 | tf_op jit(solution)/shard_map/reduce_scatter | solution.py:101
  37.7 0.7 copy-start.1
  41.7 0.7 copy-start.5
  41.7 0.9 copy-start.2
  44.3 168.6 %all-to-all-start.1 = ((bf16[24,513,80]{1,2,0:T(8,128)(2,1)}), bf16[24,513,80]{1,2,0:T(8,128)(2,1)}, u32[]{:S(2)}, u32[]{:S(2)}) async-start(bf16[24,513,80]{1,2,0:T(8,128)(2,1)} %broadcast_in_dim.15), calls=%async_computation.1 | async-start | bytes 4915200 | tf_op jit(solution)/shard_map/all_to_all | solution.py:62
  194.2 6.7 %collective-permute-start = (f32[513,80]{0,1:T(8,128)}, f32[513,80]{0,1:T(8,128)S(1)}, u32[]{:S(2)}, u32[]{:S(2)}) collective-permute-start(f32[513,80]{0,1:T(8,128)} %reduce-scatter.2.cloned.1.call-done), channel_id=1, source_target_pairs={{0,24},{24,0},{48,72},{72,48},{96,120},{120,96},{144,168},{168,144... | collective-permute-start | bytes 492488 | tf_op jit(solution)/shard_map/ppermute | solution.py:105
  201.8 8.6 %collective-permute-start.1 = (f32[513,80]{0,1:T(8,128)S(1)}, f32[513,80]{0,1:T(8,128)S(1)}, u32[]{:S(2)}, u32[]{:S(2)}) collective-permute-start(f32[513,80]{0,1:T(8,128)S(1)} %add.117), channel_id=1, source_target_pairs={{0,48},{24,72},{48,0},{72,24},{96,144},{120,168},{144,96},{168,120... | collective-permute-start | bytes 492488 | tf_op jit(solution)/shard_map/ppermute | solution.py:105
  210.4 8.2 %collective-permute-start.2 = (f32[513,80]{0,1:T(8,128)S(1)}, f32[513,80]{0,1:T(8,128)S(1)}, u32[]{:S(2)}, u32[]{:S(2)}) collective-permute-start(f32[513,80]{0,1:T(8,128)S(1)} %add.118), channel_id=1, source_target_pairs={{0,96},{24,120},{48,144},{72,168},{96,0},{120,24},{144,48},{168,72... | collective-permute-start | bytes 492488 | tf_op jit(solution)/shard_map/ppermute | solution.py:105
  219.3 15.3 %collective-permute-start.3 = (f32[513,80]{0,1:T(8,128)}, f32[513,80]{0,1:T(8,128)}, u32[]{:S(2)}, u32[]{:S(2)}) collective-permute-start(f32[513,80]{0,1:T(8,128)} %add.119), channel_id=1, source_target_pairs={{0,192},{24,216},{48,240},{72,264},{96,288},{120,312},{144,336},{1... | collective-permute-start | bytes 492488 | tf_op jit(solution)/shard_map/ppermute | solution.py:105
  230.6 9.2 %copy-start.3 = (f32[1920]{0:T(1024)S(1)}, f32[1920]{0:T(1024)}, u32[]{:S(2)}) copy-start(f32[1920]{0:T(1024)} %reshape.139) | copy-start | bytes 23044
  235.7 16.8 %collective-permute-start.4 = (f32[513,80]{0,1:T(8,128)S(1)}, f32[513,80]{0,1:T(8,128)S(1)}, u32[]{:S(2)}, u32[]{:S(2)}) collective-permute-start(f32[513,80]{0,1:T(8,128)S(1)} %add.120), channel_id=1, source_target_pairs={{0,384},{24,408},{48,432},{72,456},{96,480},{120,504},{144,528},{1... | collective-permute-start | bytes 492488 | tf_op jit(solution)/shard_map/ppermute | solution.py:105
Sparse Core Ops, SparseCore 0:
  41.8 152.3 reduce-scatter.1

commit v3 on v1

--- a/solution.py
+++ b/solution.py
@@ -39,7 +39,7 @@
     ).astype(jnp.bfloat16)
 
 
-def local(
+def step(
     waveform,
     destination,
     lengths,
@@ -57,10 +57,6 @@
     frame_count = cotangent.shape[1]
     d_conv = proj_weight.shape[0]
     slot_cap = slot_count // dp_size
-    weight_and_bias = lax.all_gather(
-        jnp.concatenate([proj_weight, proj_bias[None, :]], axis=0), "fsdp", axis=1, tiled=True
-    )
-    weights, biases = weight_and_bias[:d_conv], weight_and_bias[d_conv]
     targets = destination[:, 0]
     row_order = jnp.arange(row_count, dtype=jnp.int32)
     same_dest = targets[:, None] == targets[None, :]
@@ -82,20 +78,46 @@
     frame_ids = jnp.arange(frame_count, dtype=jnp.float32)
     valid = (10 * frame_ids[None, :] + 20 <= got_length[:, None]).reshape(-1, 1)
     frame_mask = valid.astype(jnp.float32)
-    projected = jnp.dot(normed, weights, preferred_element_type=jnp.float32) + biases.astype(
-        jnp.float32
-    )
-    features = (projected * frame_mask).astype(jnp.bfloat16).reshape(slot_count, frame_count, -1)
     cot_rows = cotangent.reshape(slot_count * frame_count, -1)
     grad_out = jnp.where(valid, cot_rows, jnp.zeros_like(cot_rows))
     normed_ext = jnp.concatenate([normed, jnp.ones((normed.shape[0], 1), normed.dtype)], axis=1)
     grad_term = lax.dot_general(
         normed_ext, grad_out, (((0,), (0,)), ((), ())), preferred_element_type=jnp.float32
     )
+    fsdp_size = lax.axis_size("fsdp")
+    own_block = jnp.concatenate([proj_weight, proj_bias[None, :]], axis=0)
+    own_block, grad_term = lax.optimization_barrier((own_block, grad_term))
+    blocks = lax.all_to_all(
+        jnp.broadcast_to(own_block[None], (fsdp_size,) + own_block.shape),
+        "fsdp",
+        split_axis=0,
+        concat_axis=0,
+        tiled=True,
+    )
+    weights, biases = blocks[:, :d_conv], blocks[:, d_conv].reshape(-1)
     part = lax.psum_scatter(grad_term, "fsdp", scatter_dimension=1, tiled=True)
-    total = lax.reduce_precision(lax.psum(part, "dp"), exponent_bits=8, mantissa_bits=7)
+    projected = jnp.einsum(
+        "rc,jcn->rjn", normed, weights, preferred_element_type=jnp.float32
+    ).reshape(normed.shape[0], -1) + biases.astype(jnp.float32)
+    features = (projected * frame_mask).astype(jnp.bfloat16).reshape(slot_count, frame_count, -1)
+
+    rows = part.shape[0]
+    piece_rows = -(-rows // dp_size)
+    padded = jnp.pad(part, ((0, piece_rows * dp_size - rows), (0, 0)))
+    pieces = lax.all_to_all(
+        padded.reshape(dp_size, piece_rows, -1), "dp", split_axis=0, concat_axis=0, tiled=True
+    )
+    reduced = jnp.sum(pieces, axis=0).astype(jnp.bfloat16)
+    gathered = lax.all_to_all(
+        jnp.broadcast_to(reduced[None], (dp_size,) + reduced.shape),
+        "dp",
+        split_axis=0,
+        concat_axis=0,
+        tiled=True,
+    )
+    total = gathered.reshape(piece_rows * dp_size, -1)[:rows]
     grad_weight, grad_bias = total[:d_conv], total[d_conv]
-    return (features, grad_weight.astype(jnp.bfloat16), grad_bias.astype(jnp.bfloat16))
+    return (features, grad_weight, grad_bias)
 
 
 def solution(mesh):
@@ -112,4 +134,4 @@
         P(("dp", "fsdp"), None, None),
     )
     out_specs = (P(("dp", "fsdp"), None, None), P(None, "fsdp"), P("fsdp"))
-    return jax.shard_map(local, mesh=mesh, in_specs=in_specs, out_specs=out_specs, check_vma=False)
+    return jax.shard_map(step, mesh=mesh, in_specs=in_specs, out_specs=out_specs, check_vma=False)

time: 363 us -> 258 us (0.71)
  the two profiles are of different devices: /device:TPU:2 before, /device:TPU:8 now
where the time goes in v3:
time: 258 us; the launch traced here: 257 us
  waiting for transfers between devices  146 us (57%)
  starting transfers between devices  41.7 us (16%)
  local copies, waits for them, and re-layouts  30.8 us (12%)
  other arithmetic  18.2 us (7%)
  between operations  14.3 us (6%)
  matrix products  5.59 us (2%)
    unnamed x2, waiting for transfers between devices  135 us
    unnamed x15, local copies, waits for them, and re-layouts  14.1 us
    all_to_all x1, starting transfers between devices, step(): lax.all_to_all(slot_rows.reshape(dp_size, slot_cap, -1), 'dp', split_axis...  12.9 us
    all_to_all x1, starting transfers between devices, step(): lax.all_to_all(jnp.broadcast_to(own_block[None], (fsdp_size,) + own_block...  12.6 us
    all_to_all x1, starting transfers between devices, step(): lax.all_to_all(jnp.broadcast_to(reduced[None], (dp_size,) + reduced.shape...  9.31 us
    all_to_all x1, waiting for transfers between devices, step(): lax.all_to_all(jnp.broadcast_to(reduced[None], (dp_size,) + reduced.shape...  7.13 us
    all_to_all x1, starting transfers between devices, step(): lax.all_to_all(padded.reshape(dp_size, piece_rows, -1), 'dp', split_axis=...  6.81 us
  transfers between devices with their start and end apart: 5, of which 4 were waited for; matrix products, arithmetic and copies ran while one was open for 8% of the time, Pallas kernels for 0%

profile of v3, /device:TPU:8, one launch (start us, length us, event | category | flops | bytes accessed | tf_op | source)
XLA Modules:
  0.0 256.9 jit_solution(483145434455110943)
XLA Ops:
  7.2 0.8 convert_bitcast_fusion
  8.0 0.9 convert_reduce_fusion.3
  8.9 0.7 multiply_add_fusion.3
  9.6 1.0 convolution_convert_fusion
  10.6 0.7 copy.35
  11.3 12.9 %all-to-all-start = ((bf16[32,2,51]{2,1,0:T(2,128)(2,1)}), bf16[32,2,51]{2,1,0:T(2,128)(2,1)S(1)}, u32[]{:S(2)}, u32[]{:S(2)}) async-start(bf16[32,2,51]{2,1,0:T(2,128)(2,1)} %bitcast.2), calls=%async_computation | async-start | bytes 32768 | tf_op jit(solution)/shard_map/all_to_all | solution.py:71
  24.3 0.8 fusion.49
  25.1 0.8 fusion.50
  25.9 0.8 copy.39
  26.7 0.9 pad_maximum_fusion
  27.6 1.7 reshape.145
  29.3 3.5 %all-to-all-done = bf16[32,2,51]{2,1,0:T(2,128)(2,1)S(1)} async-done(((bf16[32,2,51]{2,1,0:T(2,128)(2,1)}), bf16[32,2,51]{2,1,0:T(2,128)(2,1)S(1)}, u32[]{:S(2)}, u32[]{:S(2)}) %all-to-all-start) | async-done | bytes 6560 | tf_op jit(solution)/shard_map/all_to_all | solution.py:71
  33.1 0.7 fusion.46
  34.5 0.5 fusion.51
  35.0 0.3 multiply_reduce_fusion
  35.4 4.5 %fusion.2 = bf16[768,512]{1,0:T(8,128)(2,1)S(1)} fusion(f32[768,512]{1,0:T(8,128)S(1)} %get-tuple-element.33, f32[512]{0:T(512)S(1)} %bitcast.43, f32[512]{0:T(512)S(1)} %bitcast.42, f32[768]{0:T(1024)S(1)} %add_rsqrt_fusion, f32[768]{0:T(1024)S(1)} %broadcast_multiply_fusion), kind=kLoop, calls=%fused_computation.4 | loop fusion | flops 27131904 | bytes 2369536 | tf_op jit(solution)/shard_map/convert_element_type | solution.py:28
  39.8 0.6 fusion.52
  40.5 0.2 multiply_reduce_fusion.1
  40.7 1.4 convert_reduce_fusion.1
  42.1 0.2 fusion.15
  42.4 0.2 fusion.18
  42.6 0.7 copy-done.1
  43.3 2.8 %fusion.10 = f32[513,1920]{1,0:T(8,128)} fusion(bf16[256,1920]{1,0:T(8,128)(2,1)S(1)} %reshape.145, pred[256]{0:T(512)(128)(4,1)S(1)} %le.34, bf16[256,512]{1,0:T(8,128)(2,1)S(1)} %fusion.18), kind=kOutput, calls=%fused_computation.25 | convolution fusion | flops 504791040 | bytes 5185280 | tf_op jit(solution)/shard_map/dot_general | solution.py:84
  46.0 5.8 %copy.42 = f32[513,1920]{0,1:T(8,128)} copy(f32[513,1920]{1,0:T(8,128)} %fusion.10) | data formatting | bytes 7879680
  51.9 1.7 broadcast_in_dim.22
  53.6 12.6 %all-to-all-start.1 = ((bf16[24,513,80]{1,2,0:T(8,128)(2,1)}), bf16[24,513,80]{1,2,0:T(8,128)(2,1)}, u32[]{:S(2)}, u32[]{:S(2)}) async-start(bf16[24,513,80]{1,2,0:T(8,128)(2,1)} %broadcast_in_dim.22), calls=%async_computation.1 | async-start | bytes 4915200 | tf_op jit(solution)/shard_map/all_to_all | solution.py:90
  66.2 135.2 %reduce-scatter.4.cloned.1.call-done = f32[80,513]{1,0:T(8,128)} async-done(((f32[1920,513]{1,0:T(8,128)}), f32[80,513]{1,0:T(8,128)}) %reduce-scatter.4.cloned.1.call-update) | async-done | bytes 164176
  201.4 1.1 copy.43
  202.5 1.0 reshape.158
  203.5 6.8 %all-to-all-start.2 = ((f32[32,1,1360]{2,1,0:T(1,128)}), f32[32,1,1360]{2,1,0:T(1,128)}, u32[]{:S(2)}, u32[]{:S(2)}) async-start(f32[32,1,1360]{2,1,0:T(1,128)} %reshape.158), calls=%async_computation.2 | async-start | bytes 360448 | tf_op jit(solution)/shard_map/all_to_all | solution.py:107
  210.3 1.3 convert_reduce_fusion
  211.7 1.7 slice.67
  213.5 0.7 fusion.53
  214.2 2.3 copy.40
  216.5 3.4 %reshape.146 = f32[64,4,1920]{2,1,0:T(4,128)S(1)} reshape(f32[256,24,80]{2,1,0:T(8,128)} %copy.40) | data formatting | bytes 3932160 | tf_op jit(solution)/shard_map/reshape | solution.py:101
  219.9 0.5 all-to-all-done.2
  220.4 0.5 broadcast.126
  220.9 2.7 %reduce.4 = f32[32,1360]{1,0:T(8,128)} reduce(f32[32,1,1360]{2,1,0:T(1,128)} %all-to-all-done.2, f32[]{:T(128)} %broadcast.126), dimensions={1}, to_apply=%all_to_all.14.reduce_sub_computation | reduce | bytes 348164 | tf_op jit(solution)/shard_map/all_to_all | solution.py:107
  223.6 1.8 reshape.159
  225.4 1.0 reduce_sum.79
  226.4 0.7 broadcast_in_dim.23
  227.2 1.8 reshape.160
  228.9 9.3 %all-to-all-start.3 = ((bf16[32,2,680]{2,1,0:T(2,128)(2,1)}), bf16[32,2,680]{2,1,0:T(2,128)(2,1)}, u32[]{:S(2)}, u32[]{:S(2)}) async-start(bf16[32,2,680]{2,1,0:T(2,128)(2,1)} %reshape.160), calls=%async_computation.3 | async-start | bytes 196608 | tf_op jit(solution)/shard_map/all_to_all | solution.py:111
  238.2 2.2 multiply_convert_fusion
  240.4 7.1 %all-to-all-done.3 = bf16[32,2,680]{2,1,0:T(2,128)(2,1)} async-done(((bf16[32,2,680]{2,1,0:T(2,128)(2,1)}), bf16[32,2,680]{2,1,0:T(2,128)(2,1)}, u32[]{:S(2)}, u32[]{:S(2)}) %all-to-all-start.3) | async-done | bytes 87072 | tf_op jit(solution)/shard_map/all_to_all | solution.py:111
  247.6 1.1 reshape.161
  248.8 0.5 slice_bitcast_fusion
  249.3 0.7 copy.41
  (32 shorter events, 1.4 us)
Async XLA Ops:
  7.2 32.7 %copy-start = (bf16[1536,512]{1,0:T(8,128)(2,1)S(1)}, bf16[1536,512]{1,0:T(8,128)(2,1)}, u32[]{:S(2)}) copy-start(bf16[1536,512]{1,0:T(8,128)(2,1)} %param.14) | copy-start | bytes 4718596
  7.2 27.3 %copy-start.3 = (bf16[10,512]{1,0:T(8,128)(2,1)S(1)}, bf16[10,512]{1,0:T(8,128)(2,1)}, u32[]{:S(2)}) copy-start(bf16[10,512]{1,0:T(8,128)(2,1)} %param.13) | copy-start | bytes 30724
  11.3 21.5 %all-to-all-start = ((bf16[32,2,51]{2,1,0:T(2,128)(2,1)}), bf16[32,2,51]{2,1,0:T(2,128)(2,1)S(1)}, u32[]{:S(2)}, u32[]{:S(2)}) async-start(bf16[32,2,51]{2,1,0:T(2,128)(2,1)} %bitcast.2), calls=%async_computation | async-start | bytes 32768 | tf_op jit(solution)/shard_map/all_to_all | solution.py:71
  24.3 177.1 %reduce-scatter.4.cloned.1.call-start = ((), (), s32[]{:S(2)}) async-start(), calls=%async_computation.5 | async-start | bytes 5120000
  42.6 0.7 copy-start.1
  53.6 150.0 %all-to-all-start.1 = ((bf16[24,513,80]{1,2,0:T(8,128)(2,1)}), bf16[24,513,80]{1,2,0:T(8,128)(2,1)}, u32[]{:S(2)}, u32[]{:S(2)}) async-start(bf16[24,513,80]{1,2,0:T(8,128)(2,1)} %broadcast_in_dim.22), calls=%async_computation.1 | async-start | bytes 4915200 | tf_op jit(solution)/shard_map/all_to_all | solution.py:90
  203.5 16.9 %all-to-all-start.2 = ((f32[32,1,1360]{2,1,0:T(1,128)}), f32[32,1,1360]{2,1,0:T(1,128)}, u32[]{:S(2)}, u32[]{:S(2)}) async-start(f32[32,1,1360]{2,1,0:T(1,128)} %reshape.158), calls=%async_computation.2 | async-start | bytes 360448 | tf_op jit(solution)/shard_map/all_to_all | solution.py:107
  211.7 1.7 copy-start.2
  228.9 18.7 %all-to-all-start.3 = ((bf16[32,2,680]{2,1,0:T(2,128)(2,1)}), bf16[32,2,680]{2,1,0:T(2,128)(2,1)}, u32[]{:S(2)}, u32[]{:S(2)}) async-start(bf16[32,2,680]{2,1,0:T(2,128)(2,1)} %reshape.160), calls=%async_computation.3 | async-start | bytes 196608 | tf_op jit(solution)/shard_map/all_to_all | solution.py:111
Sparse Core Ops, SparseCore 0:
  52.0 149.3 reduce-scatter.3

commit v4 on v3

--- a/solution.py
+++ b/solution.py
@@ -84,18 +84,23 @@
     grad_term = lax.dot_general(
         normed_ext, grad_out, (((0,), (0,)), ((), ())), preferred_element_type=jnp.float32
     )
-    fsdp_size = lax.axis_size("fsdp")
+    fsdp_size = lax.axis_size("z") * lax.axis_size("core")
     own_block = jnp.concatenate([proj_weight, proj_bias[None, :]], axis=0)
-    own_block, grad_term = lax.optimization_barrier((own_block, grad_term))
     blocks = lax.all_to_all(
         jnp.broadcast_to(own_block[None], (fsdp_size,) + own_block.shape),
-        "fsdp",
+        ("z", "core"),
         split_axis=0,
         concat_axis=0,
         tiled=True,
     )
     weights, biases = blocks[:, :d_conv], blocks[:, d_conv].reshape(-1)
-    part = lax.psum_scatter(grad_term, "fsdp", scatter_dimension=1, tiled=True)
+    cores = lax.axis_size("core")
+    core = lax.axis_index("core")
+    by_core = grad_term.reshape(grad_term.shape[0], -1, cores, proj_weight.shape[1])
+    mine = lax.dynamic_index_in_dim(by_core, core, axis=2, keepdims=False)
+    other = lax.dynamic_index_in_dim(by_core, cores - 1 - core, axis=2, keepdims=False)
+    pair_sum = mine + lax.ppermute(other, "core", [(0, 1), (1, 0)])
+    part = lax.psum_scatter(pair_sum, "z", scatter_dimension=1, tiled=True)[:, 0]
     projected = jnp.einsum(
         "rc,jcn->rjn", normed, weights, preferred_element_type=jnp.float32
     ).reshape(normed.shape[0], -1) + biases.astype(jnp.float32)
@@ -121,17 +126,20 @@
 
 
 def solution(mesh):
+    n_dp, n_fsdp = mesh.shape["dp"], mesh.shape["fsdp"]
+    mesh = jax.sharding.Mesh(mesh.devices.reshape(n_dp, n_fsdp // 2, 2), ("dp", "z", "core"))
+    rows = P(("dp", "z", "core"))
     in_specs = (
-        P(("dp", "fsdp"), None),
-        P(("dp", "fsdp"), None),
-        P(("dp", "fsdp")),
+        P(("dp", "z", "core"), None),
+        P(("dp", "z", "core"), None),
+        rows,
         P(),
         P(),
         P(),
         P(),
-        P(None, "fsdp"),
-        P("fsdp"),
-        P(("dp", "fsdp"), None, None),
+        P(None, ("z", "core")),
+        P(("z", "core")),
+        P(("dp", "z", "core"), None, None),
     )
-    out_specs = (P(("dp", "fsdp"), None, None), P(None, "fsdp"), P("fsdp"))
+    out_specs = (P(("dp", "z", "core"), None, None), P(None, ("z", "core")), P(("z", "core")))
     return jax.shard_map(step, mesh=mesh, in_specs=in_specs, out_specs=out_specs, check_vma=False)

time: 258 us -> 242 us (0.938)
  waiting for transfers between devices: 146 us -> 118 us
  other arithmetic: 18.2 us -> 23.2 us
  local copies, waits for them, and re-layouts: 30.8 us -> 35.8 us
    unnamed x2 -> x1, waiting for transfers between devices: 135 us -> 0.02 us
    all_to_all x1, waiting for transfers between devices: 0.01 us -> 98.7 us  [step(): lax.all_to_all(jnp.broadcast_to(own_block[None], (fsdp_size,) + own_block...]
    reduce_scatter x0 -> x1, waiting for transfers between devices: none -> 6.76 us  [step(): lax.psum_scatter(pair_sum, 'z', scatter_dimension=1, tiled=True)[:, 0]]
    add x0 -> x1, other arithmetic: none -> 4.15 us  [step(): pair_sum = mine + lax.ppermute(other, 'core', [(0, 1), (1, 0)])]
    unnamed x15 -> x22, local copies, waits for them, and re-layouts: 14.1 us -> 11.8 us
  transfers between devices with their start and end apart: 5 -> 6, of which waited for: 4 -> 4; matrix products, arithmetic and copies ran while one was open for 8% -> 10% of each run, Pallas kernels for 0% -> 0%
where the time goes in v4:
time: 242 us; the launch traced here: 241 us
  waiting for transfers between devices  118 us (49%)
  starting transfers between devices  44 us (18%)
  local copies, waits for them, and re-layouts  35.8 us (15%)
  other arithmetic  23.2 us (10%)
  between operations  14.4 us (6%)
  matrix products  6.02 us (2%)
    all_to_all x1, waiting for transfers between devices, step(): lax.all_to_all(jnp.broadcast_to(own_block[None], (fsdp_size,) + own_block...  98.7 us
    all_to_all x1, starting transfers between devices, step(): lax.all_to_all(slot_rows.reshape(dp_size, slot_cap, -1), 'dp', split_axis...  12.9 us
    all_to_all x1, starting transfers between devices, step(): lax.all_to_all(jnp.broadcast_to(own_block[None], (fsdp_size,) + own_block...  12.7 us
    unnamed x22, local copies, waits for them, and re-layouts  11.8 us
    all_to_all x1, starting transfers between devices, step(): lax.all_to_all(jnp.broadcast_to(reduced[None], (dp_size,) + reduced.shape...  9.82 us
    all_to_all x1, waiting for transfers between devices, step(): lax.all_to_all(jnp.broadcast_to(reduced[None], (dp_size,) + reduced.shape...  7.12 us
    reduce_scatter x1, waiting for transfers between devices, step(): lax.psum_scatter(pair_sum, 'z', scatter_dimension=1, tiled=True)[:, 0]  6.76 us
    all_to_all x1, starting transfers between devices, step(): lax.all_to_all(padded.reshape(dp_size, piece_rows, -1), 'dp', split_axis=...  6.63 us
  transfers between devices with their start and end apart: 6, of which 4 were waited for; matrix products, arithmetic and copies ran while one was open for 10% of the time, Pallas kernels for 0%

profile of v4, /device:TPU:8, one launch (start us, length us, event | category | flops | bytes accessed | tf_op | source)
XLA Modules:
  0.0 241.2 jit_solution(893527028090495378)
XLA Ops:
  7.2 0.8 convert_bitcast_fusion
  8.1 0.9 convert_reduce_fusion.3
  9.0 0.7 multiply_add_fusion.3
  9.7 1.0 convolution_convert_fusion
  10.6 0.7 copy.45
  11.3 12.9 %all-to-all-start = ((bf16[32,2,51]{2,1,0:T(2,128)(2,1)}), bf16[32,2,51]{2,1,0:T(2,128)(2,1)S(1)}, u32[]{:S(2)}, u32[]{:S(2)}) async-start(bf16[32,2,51]{2,1,0:T(2,128)(2,1)} %bitcast.2), calls=%async_computation | async-start | bytes 32768 | tf_op jit(solution)/shard_map/all_to_all | solution.py:71
  24.3 0.8 fusion.46
  25.1 0.8 fusion.47
  25.9 1.7 reshape.148
  27.6 5.2 %all-to-all-done = bf16[32,2,51]{2,1,0:T(2,128)(2,1)S(1)} async-done(((bf16[32,2,51]{2,1,0:T(2,128)(2,1)}), bf16[32,2,51]{2,1,0:T(2,128)(2,1)S(1)}, u32[]{:S(2)}, u32[]{:S(2)}) %all-to-all-start) | async-done | bytes 6560 | tf_op jit(solution)/shard_map/all_to_all | solution.py:71
  34.5 4.5 %fusion.2 = bf16[768,512]{1,0:T(8,128)(2,1)S(1)} fusion(f32[768,512]{1,0:T(8,128)S(1)} %get-tuple-element.29, f32[512]{0:T(512)S(1)} %bitcast.53, f32[512]{0:T(512)S(1)} %bitcast.52, f32[768]{0:T(1024)S(1)} %add_rsqrt_fusion, f32[768]{0:T(1024)S(1)} %broadcast_multiply_fusion), kind=kLoop, calls=%fused_computation.6 | loop fusion | flops 27131904 | bytes 2369536 | tf_op jit(solution)/shard_map/convert_element_type | solution.py:28
  39.9 1.4 convert_reduce_fusion.1
  41.3 0.7 copy-done.3
  42.3 0.7 broadcast_compare_fusion
  43.6 0.8 select_bitcast_fusion
  44.4 0.6 copy.51
  45.1 1.1 fusion.15
  46.2 0.7 copy-done.2
  46.9 0.9 fusion.26
  47.9 1.8 dynamic-slice_bitcast_fusion
  49.7 1.1 copy-done.1
  50.8 1.9 collective-permute-start
  52.9 1.7 broadcast_in_dim.17
  54.6 12.7 %all-to-all-start.1 = ((bf16[24,513,80]{1,2,0:T(8,128)(2,1)}), bf16[24,513,80]{1,2,0:T(8,128)(2,1)}, u32[]{:S(2)}, u32[]{:S(2)}) async-start(bf16[24,513,80]{1,2,0:T(8,128)(2,1)} %broadcast_in_dim.17), calls=%async_computation.1 | async-start | bytes 4915200 | tf_op jit(solution)/shard_map/all_to_all | solution.py:89
  67.3 4.2 %bitcast_add_fusion = f32[513,12,80]{0,2,1:T(8,128)} fusion(f32[513,12,80]{0,2,1:T(8,128)} %collective-permute-done, f32[513,12,2,80]{0,3,2,1:T(8,128)} %copy-done.1, s32[]{:T(128)S(6)} %select_n.12), kind=kLoop, calls=%fused_computation | loop fusion | flops 492480 | bytes 5909764 | tf_op jit(solution)/shard_map/add | solution.py:102
  71.5 98.7 %all-to-all-done.1 = bf16[24,513,80]{1,2,0:T(8,128)(2,1)} async-done(((bf16[24,513,80]{1,2,0:T(8,128)(2,1)}), bf16[24,513,80]{1,2,0:T(8,128)(2,1)}, u32[]{:S(2)}, u32[]{:S(2)}) %all-to-all-start.1) | async-done | bytes 1969952 | tf_op jit(solution)/shard_map/all_to_all | solution.py:89
  170.2 1.7 slice.66
  171.9 6.8 %reduce-scatter.2.cloned.1.call-done = f32[513,1,80]{0,2,1:T(8,128)} async-done(((f32[513,12,80]{0,2,1:T(8,128)}), f32[513,1,80]{0,2,1:T(8,128)}) %reduce-scatter.2.cloned.1.call-update) | async-done | bytes 164176 | tf_op jit(solution)/shard_map/reduce_scatter | solution.py:103
  178.7 1.8 copy.57
  180.4 1.7 pad.5.clone
  182.1 1.7 reshape.149
  183.8 2.0 reshape.159
  185.8 6.6 %all-to-all-start.2 = ((f32[32,1,1360]{2,1,0:T(1,128)}), f32[32,1,1360]{2,1,0:T(1,128)}, u32[]{:S(2)}, u32[]{:S(2)}) async-start(f32[32,1,1360]{2,1,0:T(1,128)} %reshape.159), calls=%async_computation.3 | async-start | bytes 360448 | tf_op jit(solution)/shard_map/all_to_all | solution.py:112
  192.5 3.0 %fusion.50 = f32[256,1920]{0,1} fusion(bf16[256,512]{1,0:T(8,128)(2,1)} %copy-done.2, bf16[512,1920]{0,1:T(8,128)(2,1)S(1)} %bitcast.42), kind=kOutput, calls=%fused_computation.96 | convolution fusion | flops 503316480 | bytes 4194304
  195.5 3.3 %copy.50 = f32[256,24,80]{2,1,0:T(8,128)} copy(f32[256,24,80]{0,2,1:T(8,128)} %bitcast.43) | data formatting | bytes 3932160 | tf_op jit(solution)/shard_map/rc,jcn->rjn/dot_general | solution.py:104
  198.8 3.4 %reshape.147 = f32[64,4,1920]{2,1,0:T(4,128)S(1)} reshape(f32[256,24,80]{2,1,0:T(8,128)} %copy.50) | data formatting | bytes 3932160 | tf_op jit(solution)/shard_map/reshape | solution.py:106
  202.2 1.3 convert_reduce_fusion
  203.5 0.7 reshape.151
  204.7 2.7 %reduce.4 = f32[32,1360]{1,0:T(8,128)} reduce(f32[32,1,1360]{2,1,0:T(1,128)} %all-to-all-done.2, f32[]{:T(128)} %broadcast.126), dimensions={1}, to_apply=%all_to_all.14.reduce_sub_computation | reduce | bytes 348164 | tf_op jit(solution)/shard_map/all_to_all | solution.py:112
  207.4 1.8 reshape.160
  209.2 1.0 reduce_sum.79
  210.3 0.7 broadcast_in_dim.23
  211.0 1.8 reshape.161
  212.7 9.8 %all-to-all-start.3 = ((bf16[32,2,680]{2,1,0:T(2,128)(2,1)}), bf16[32,2,680]{2,1,0:T(2,128)(2,1)}, u32[]{:S(2)}, u32[]{:S(2)}) async-start(bf16[32,2,680]{2,1,0:T(2,128)(2,1)} %reshape.161), calls=%async_computation.4 | async-start | bytes 196608 | tf_op jit(solution)/shard_map/all_to_all | solution.py:116
  222.6 2.2 multiply_convert_fusion
  224.8 7.1 %all-to-all-done.3 = bf16[32,2,680]{2,1,0:T(2,128)(2,1)} async-done(((bf16[32,2,680]{2,1,0:T(2,128)(2,1)}), bf16[32,2,680]{2,1,0:T(2,128)(2,1)}, u32[]{:S(2)}, u32[]{:S(2)}) %all-to-all-start.3) | async-done | bytes 87072 | tf_op jit(solution)/shard_map/all_to_all | solution.py:116
  231.9 1.1 reshape.162
  233.6 0.7 copy.54
  (45 shorter events, 4.8 us)
Async XLA Ops:
  7.2 31.9 %copy-start = (bf16[1536,512]{1,0:T(8,128)(2,1)S(1)}, bf16[1536,512]{1,0:T(8,128)(2,1)}, u32[]{:S(2)}) copy-start(bf16[1536,512]{1,0:T(8,128)(2,1)} %param.14) | copy-start | bytes 4718596
  7.2 26.5 %copy-start.6 = (bf16[10,512]{1,0:T(8,128)(2,1)S(1)}, bf16[10,512]{1,0:T(8,128)(2,1)}, u32[]{:S(2)}) copy-start(bf16[10,512]{1,0:T(8,128)(2,1)} %param.13) | copy-start | bytes 30724
  11.3 21.5 %all-to-all-start = ((bf16[32,2,51]{2,1,0:T(2,128)(2,1)}), bf16[32,2,51]{2,1,0:T(2,128)(2,1)S(1)}, u32[]{:S(2)}, u32[]{:S(2)}) async-start(bf16[32,2,51]{2,1,0:T(2,128)(2,1)} %bitcast.2), calls=%async_computation | async-start | bytes 32768 | tf_op jit(solution)/shard_map/all_to_all | solution.py:71
  41.3 0.7 copy-start.3
  46.2 0.7 copy-start.2
  47.9 3.0 %copy-start.1 = (f32[513,12,2,80]{0,3,2,1:T(8,128)}, f32[513,12,2,80]{0,3,2,1:T(8,128)S(1)}, u32[]{:S(2)}) copy-start(f32[513,12,2,80]{0,3,2,1:T(8,128)S(1)} %fusion.26) | copy-start | bytes 11819524
  47.9 4.9 %copy-start.7 = (bf16[80]{0:T(256)(128)(2,1)S(1)}, bf16[80]{0:T(256)(128)(2,1)}, u32[]{:S(2)}) copy-start(bf16[80]{0:T(256)(128)(2,1)} %param.18) | copy-start | bytes 484
  47.9 5.0 %copy-start.4 = (bf16[512,80]{0,1:T(8,128)(2,1)S(1)}, bf16[512,80]{0,1:T(8,128)(2,1)}, u32[]{:S(2)}) copy-start(bf16[512,80]{0,1:T(8,128)(2,1)} %param.17) | copy-start | bytes 245764
  50.8 16.5 %collective-permute-start = (f32[513,12,80]{0,2,1:T(8,128)}, f32[513,12,80]{0,2,1:T(8,128)}, u32[]{:S(2)}, u32[]{:S(2)}) collective-permute-start(f32[513,12,80]{0,2,1:T(8,128)} %dynamic-slice_bitcast_fusion), channel_id=1, source_target_pairs={{0,1},{1,0},{2,3},{3,2},{4,5},{5,4},{6,7},{7,6},{8,9},{9,8},{10,11... | collective-permute-start | bytes 5909768 | tf_op jit(solution)/shard_map/ppermute | solution.py:102
  54.6 115.6 %all-to-all-start.1 = ((bf16[24,513,80]{1,2,0:T(8,128)(2,1)}), bf16[24,513,80]{1,2,0:T(8,128)(2,1)}, u32[]{:S(2)}, u32[]{:S(2)}) async-start(bf16[24,513,80]{1,2,0:T(8,128)(2,1)} %broadcast_in_dim.17), calls=%async_computation.1 | async-start | bytes 4915200 | tf_op jit(solution)/shard_map/all_to_all | solution.py:89
  67.3 111.4 %reduce-scatter.2.cloned.1.call-start = ((), (), s32[]{:S(2)}) async-start(), calls=%async_computation.5 | async-start | bytes 2662400 | tf_op jit(solution)/shard_map/reduce_scatter | solution.py:103
  185.8 18.4 %all-to-all-start.2 = ((f32[32,1,1360]{2,1,0:T(1,128)}), f32[32,1,1360]{2,1,0:T(1,128)}, u32[]{:S(2)}, u32[]{:S(2)}) async-start(f32[32,1,1360]{2,1,0:T(1,128)} %reshape.159), calls=%async_computation.3 | async-start | bytes 360448 | tf_op jit(solution)/shard_map/all_to_all | solution.py:112
  204.2 18.3 %copy-start.5 = (f32[1920]{0:T(1024)S(1)}, f32[1920]{0:T(1024)}, u32[]{:S(2)}) copy-start(f32[1920]{0:T(1024)} %reshape.151) | copy-start | bytes 23044
  212.7 19.2 %all-to-all-start.3 = ((bf16[32,2,680]{2,1,0:T(2,128)(2,1)}), bf16[32,2,680]{2,1,0:T(2,128)(2,1)}, u32[]{:S(2)}, u32[]{:S(2)}) async-start(bf16[32,2,680]{2,1,0:T(2,128)(2,1)} %reshape.161), calls=%async_computation.4 | async-start | bytes 196608 | tf_op jit(solution)/shard_map/all_to_all | solution.py:116
Sparse Core Ops, SparseCore 0:
  71.6 106.9 reduce-scatter.1

commit v5 on v4

--- a/solution.py
+++ b/solution.py
@@ -86,16 +86,20 @@
     )
     fsdp_size = lax.axis_size("z") * lax.axis_size("core")
     own_block = jnp.concatenate([proj_weight, proj_bias[None, :]], axis=0)
+    cores = lax.axis_size("core")
+    core = lax.axis_index("core")
+    partner_block = lax.ppermute(own_block, "core", [(0, 1), (1, 0)])
+    chip_blocks = jnp.where(
+        core == 0, jnp.stack([own_block, partner_block]), jnp.stack([partner_block, own_block])
+    )
     blocks = lax.all_to_all(
-        jnp.broadcast_to(own_block[None], (fsdp_size,) + own_block.shape),
-        ("z", "core"),
+        jnp.broadcast_to(chip_blocks[None], (fsdp_size // cores,) + chip_blocks.shape),
+        "z",
         split_axis=0,
         concat_axis=0,
         tiled=True,
-    )
+    ).reshape((fsdp_size,) + own_block.shape)
     weights, biases = blocks[:, :d_conv], blocks[:, d_conv].reshape(-1)
-    cores = lax.axis_size("core")
-    core = lax.axis_index("core")
     by_core = grad_term.reshape(grad_term.shape[0], -1, cores, proj_weight.shape[1])
     mine = lax.dynamic_index_in_dim(by_core, core, axis=2, keepdims=False)
     other = lax.dynamic_index_in_dim(by_core, cores - 1 - core, axis=2, keepdims=False)

time: 242 us -> 247 us (1.021)
  waiting for transfers between devices: 118 us -> 121 us
  transfers between devices with their start and end apart: 6 -> 7, of which waited for: 4 -> 5; matrix products, arithmetic and copies ran while one was open for 10% -> 10% of each run, Pallas kernels for 0% -> 0%
where the time goes in v5:
time: 247 us; the launch traced here: 246 us
  waiting for transfers between devices  121 us (49%)
  starting transfers between devices  46 us (19%)
  local copies, waits for them, and re-layouts  35.8 us (14%)
  other arithmetic  23.3 us (9%)
  between operations  14.4 us (6%)
  matrix products  6.02 us (2%)
    all_to_all x1, waiting for transfers between devices, step(): lax.all_to_all(jnp.broadcast_to(chip_blocks[None], (fsdp_size // cores,)...  100 us
    all_to_all x1, starting transfers between devices, step(): lax.all_to_all(slot_rows.reshape(dp_size, slot_cap, -1), 'dp', split_axis...  12.9 us
    all_to_all x1, starting transfers between devices, step(): lax.all_to_all(jnp.broadcast_to(chip_blocks[None], (fsdp_size // cores,)...  12.3 us
    unnamed x22, local copies, waits for them, and re-layouts  11.8 us
    all_to_all x1, starting transfers between devices, step(): lax.all_to_all(jnp.broadcast_to(reduced[None], (dp_size,) + reduced.shape...  9.82 us
    all_to_all x1, waiting for transfers between devices, step(): lax.all_to_all(jnp.broadcast_to(reduced[None], (dp_size,) + reduced.shape...  7.12 us
    all_to_all x1, starting transfers between devices, step(): lax.all_to_all(padded.reshape(dp_size, piece_rows, -1), 'dp', split_axis=...  6.59 us
    reduce_scatter x1, waiting for transfers between devices, step(): lax.psum_scatter(pair_sum, 'z', scatter_dimension=1, tiled=True)[:, 0]  5.48 us
  transfers between devices with their start and end apart: 7, of which 5 were waited for; matrix products, arithmetic and copies ran while one was open for 10% of the time, Pallas kernels for 0%

profile of v5, /device:TPU:8, one launch (start us, length us, event | category | flops | bytes accessed | tf_op | source)
XLA Modules:
  0.0 246.2 jit_solution(7158201557796544276)
XLA Ops:
  7.2 0.8 convert_bitcast_fusion
  8.1 0.9 convert_reduce_fusion.3
  9.7 1.0 convolution_convert_fusion
  10.6 0.7 copy.45
  11.3 12.9 %all-to-all-start = ((bf16[32,2,51]{2,1,0:T(2,128)(2,1)}), bf16[32,2,51]{2,1,0:T(2,128)(2,1)S(1)}, u32[]{:S(2)}, u32[]{:S(2)}) async-start(bf16[32,2,51]{2,1,0:T(2,128)(2,1)} %bitcast.2), calls=%async_computation | async-start | bytes 32768 | tf_op jit(solution)/shard_map/all_to_all | solution.py:71
  24.3 0.8 fusion.47
  25.1 0.8 fusion.48
  25.9 1.7 reshape.184
  27.6 5.2 %all-to-all-done = bf16[32,2,51]{2,1,0:T(2,128)(2,1)S(1)} async-done(((bf16[32,2,51]{2,1,0:T(2,128)(2,1)}), bf16[32,2,51]{2,1,0:T(2,128)(2,1)S(1)}, u32[]{:S(2)}, u32[]{:S(2)}) %all-to-all-start) | async-done | bytes 6560 | tf_op jit(solution)/shard_map/all_to_all | solution.py:71
  34.5 4.5 %fusion.2 = bf16[768,512]{1,0:T(8,128)(2,1)S(1)} fusion(f32[768,512]{1,0:T(8,128)S(1)} %get-tuple-element.31, f32[512]{0:T(512)S(1)} %bitcast.58, f32[512]{0:T(512)S(1)} %bitcast.57, f32[768]{0:T(1024)S(1)} %add_rsqrt_fusion, f32[768]{0:T(1024)S(1)} %broadcast_multiply_fusion), kind=kLoop, calls=%fused_computation.6 | loop fusion | flops 27131904 | bytes 2369536 | tf_op jit(solution)/shard_map/convert_element_type | solution.py:28
  39.9 1.4 convert_reduce_fusion.1
  41.3 0.7 copy-done.3
  42.3 0.7 broadcast_compare_fusion
  43.6 0.8 select_bitcast_fusion
  45.1 1.1 fusion.15
  46.2 0.7 copy-done.2
  46.9 0.9 fusion.26
  47.9 1.8 dynamic-slice_bitcast_fusion
  49.7 1.1 copy-done.1
  50.8 1.9 collective-permute-start.1
  52.9 2.4 collective-permute-start
  55.3 2.4 collective-permute-done
  57.8 1.7 broadcast_in_dim.17
  59.5 12.3 %all-to-all-start.1 = ((bf16[12,2,513,80]{2,3,1,0:T(8,128)(2,1)}), bf16[12,2,513,80]{2,3,1,0:T(8,128)(2,1)}, u32[]{:S(2)}, u32[]{:S(2)}) async-start(bf16[12,2,513,80]{2,3,1,0:T(8,128)(2,1)} %broadcast_in_dim.17), calls=%async_computation.1 | async-start | bytes 4915200 | tf_op jit(solution)/shard_map/all_to_all | solution.py:95
  71.8 4.2 %bitcast_add_fusion = f32[513,12,80]{0,2,1:T(8,128)} fusion(f32[513,12,80]{0,2,1:T(8,128)} %collective-permute-done.1, f32[513,12,2,80]{0,3,2,1:T(8,128)} %copy-done.1, s32[]{:T(128)S(6)} %select_n.26), kind=kLoop, calls=%fused_computation | loop fusion | flops 492480 | bytes 5909764 | tf_op jit(solution)/shard_map/add | solution.py:106
  76.0 100.5 %all-to-all-done.1 = bf16[12,2,513,80]{2,3,1,0:T(8,128)(2,1)} async-done(((bf16[12,2,513,80]{2,3,1,0:T(8,128)(2,1)}), bf16[12,2,513,80]{2,3,1,0:T(8,128)(2,1)}, u32[]{:S(2)}, u32[]{:S(2)}) %all-to-all-start.1) | async-done | bytes 1969952 | tf_op jit(solution)/shard_map/all_to_all | solution.py:95
  176.5 1.7 slice.66
  178.2 5.5 %reduce-scatter.2.cloned.1.call-done = f32[513,1,80]{0,2,1:T(8,128)} async-done(((f32[513,12,80]{0,2,1:T(8,128)}), f32[513,1,80]{0,2,1:T(8,128)}) %reduce-scatter.2.cloned.1.call-update) | async-done | bytes 164176 | tf_op jit(solution)/shard_map/reduce_scatter | solution.py:107
  183.7 1.8 copy.57
  185.5 1.7 pad.5.clone
  187.1 1.7 reshape.185
  188.9 2.0 reshape.195
  190.9 6.6 %all-to-all-start.2 = ((f32[32,1,1360]{2,1,0:T(1,128)}), f32[32,1,1360]{2,1,0:T(1,128)}, u32[]{:S(2)}, u32[]{:S(2)}) async-start(f32[32,1,1360]{2,1,0:T(1,128)} %reshape.195), calls=%async_computation.3 | async-start | bytes 360448 | tf_op jit(solution)/shard_map/all_to_all | solution.py:116
  197.5 3.0 %fusion.51 = f32[256,1920]{0,1} fusion(bf16[256,512]{1,0:T(8,128)(2,1)} %copy-done.2, bf16[512,1920]{0,1:T(8,128)(2,1)S(1)} %bitcast.46), kind=kOutput, calls=%fused_computation.98 | convolution fusion | flops 503316480 | bytes 4194304
  200.5 3.3 %copy.50 = f32[256,24,80]{2,1,0:T(8,128)} copy(f32[256,24,80]{0,2,1:T(8,128)} %bitcast.47) | data formatting | bytes 3932160 | tf_op jit(solution)/shard_map/rc,jcn->rjn/dot_general | solution.py:108
  203.8 3.4 %reshape.183 = f32[64,4,1920]{2,1,0:T(4,128)S(1)} reshape(f32[256,24,80]{2,1,0:T(8,128)} %copy.50) | data formatting | bytes 3932160 | tf_op jit(solution)/shard_map/reshape | solution.py:110
  207.2 1.3 convert_reduce_fusion
  208.5 0.7 reshape.187
  209.7 2.7 %reduce.4 = f32[32,1360]{1,0:T(8,128)} reduce(f32[32,1,1360]{2,1,0:T(1,128)} %all-to-all-done.2, f32[]{:T(128)} %broadcast.129), dimensions={1}, to_apply=%all_to_all.14.reduce_sub_computation | reduce | bytes 348164 | tf_op jit(solution)/shard_map/all_to_all | solution.py:116
  212.4 1.8 reshape.196
  214.2 1.0 reduce_sum.79
  215.3 0.7 broadcast_in_dim.23
  216.0 1.8 reshape.197
  217.7 9.8 %all-to-all-start.3 = ((bf16[32,2,680]{2,1,0:T(2,128)(2,1)}), bf16[32,2,680]{2,1,0:T(2,128)(2,1)}, u32[]{:S(2)}, u32[]{:S(2)}) async-start(bf16[32,2,680]{2,1,0:T(2,128)(2,1)} %reshape.197), calls=%async_computation.4 | async-start | bytes 196608 | tf_op jit(solution)/shard_map/all_to_all | solution.py:120
  227.6 2.2 multiply_convert_fusion
  229.8 7.1 %all-to-all-done.3 = bf16[32,2,680]{2,1,0:T(2,128)(2,1)} async-done(((bf16[32,2,680]{2,1,0:T(2,128)(2,1)}), bf16[32,2,680]{2,1,0:T(2,128)(2,1)}, u32[]{:S(2)}, u32[]{:S(2)}) %all-to-all-start.3) | async-done | bytes 87072 | tf_op jit(solution)/shard_map/all_to_all | solution.py:120
  236.9 1.1 reshape.198
  238.7 0.7 copy.54
  (48 shorter events, 6.2 us)
Async XLA Ops:
  7.2 31.9 %copy-start = (bf16[1536,512]{1,0:T(8,128)(2,1)S(1)}, bf16[1536,512]{1,0:T(8,128)(2,1)}, u32[]{:S(2)}) copy-start(bf16[1536,512]{1,0:T(8,128)(2,1)} %param.14) | copy-start | bytes 4718596
  7.2 26.5 %copy-start.6 = (bf16[10,512]{1,0:T(8,128)(2,1)S(1)}, bf16[10,512]{1,0:T(8,128)(2,1)}, u32[]{:S(2)}) copy-start(bf16[10,512]{1,0:T(8,128)(2,1)} %param.13) | copy-start | bytes 30724
  11.3 21.5 %all-to-all-start = ((bf16[32,2,51]{2,1,0:T(2,128)(2,1)}), bf16[32,2,51]{2,1,0:T(2,128)(2,1)S(1)}, u32[]{:S(2)}, u32[]{:S(2)}) async-start(bf16[32,2,51]{2,1,0:T(2,128)(2,1)} %bitcast.2), calls=%async_computation | async-start | bytes 32768 | tf_op jit(solution)/shard_map/all_to_all | solution.py:71
  41.3 0.7 copy-start.3
  46.2 0.7 copy-start.2
  47.9 2.9 %copy-start.1 = (f32[513,12,2,80]{0,3,2,1:T(8,128)}, f32[513,12,2,80]{0,3,2,1:T(8,128)S(1)}, u32[]{:S(2)}) copy-start(f32[513,12,2,80]{0,3,2,1:T(8,128)S(1)} %fusion.26) | copy-start | bytes 11819524
  47.9 4.9 %copy-start.7 = (bf16[80]{0:T(256)(128)(2,1)S(1)}, bf16[80]{0:T(256)(128)(2,1)}, u32[]{:S(2)}) copy-start(bf16[80]{0:T(256)(128)(2,1)} %param.18) | copy-start | bytes 484
  47.9 5.0 %copy-start.4 = (bf16[512,80]{0,1:T(8,128)(2,1)S(1)}, bf16[512,80]{0,1:T(8,128)(2,1)}, u32[]{:S(2)}) copy-start(bf16[512,80]{0,1:T(8,128)(2,1)} %param.17) | copy-start | bytes 245764
  50.8 21.0 %collective-permute-start.1 = (f32[513,12,80]{0,2,1:T(8,128)}, f32[513,12,80]{0,2,1:T(8,128)}, u32[]{:S(2)}, u32[]{:S(2)}) collective-permute-start(f32[513,12,80]{0,2,1:T(8,128)} %dynamic-slice_bitcast_fusion), channel_id=1, source_target_pairs={{0,1},{1,0},{2,3},{3,2},{4,5},{5,4},{6,7},{7,6},{8,9},{9,8},{10,11... | collective-permute-start | bytes 5909768 | tf_op jit(solution)/shard_map/ppermute | solution.py:106
  52.9 4.8 %collective-permute-start = (bf16[513,80]{0,1:T(8,128)(2,1)S(1)}, bf16[513,80]{0,1:T(8,128)(2,1)S(1)}, u32[]{:S(2)}, u32[]{:S(2)}) collective-permute-start(bf16[513,80]{0,1:T(8,128)(2,1)S(1)} %get-tuple-element.18), channel_id=1, source_target_pairs={{0,1},{1,0},{2,3},{3,2},{4,5},{5,4},{6,7},{7,6},{8,9},{9,8},{10,11... | collective-permute-start | bytes 246248 | tf_op jit(solution)/shard_map/ppermute | solution.py:91
  59.5 117.0 %all-to-all-start.1 = ((bf16[12,2,513,80]{2,3,1,0:T(8,128)(2,1)}), bf16[12,2,513,80]{2,3,1,0:T(8,128)(2,1)}, u32[]{:S(2)}, u32[]{:S(2)}) async-start(bf16[12,2,513,80]{2,3,1,0:T(8,128)(2,1)} %broadcast_in_dim.17), calls=%async_computation.1 | async-start | bytes 4915200 | tf_op jit(solution)/shard_map/all_to_all | solution.py:95
  71.8 111.9 %reduce-scatter.2.cloned.1.call-start = ((), (), s32[]{:S(2)}) async-start(), calls=%async_computation.5 | async-start | bytes 2662400 | tf_op jit(solution)/shard_map/reduce_scatter | solution.py:107
  190.9 18.3 %all-to-all-start.2 = ((f32[32,1,1360]{2,1,0:T(1,128)}), f32[32,1,1360]{2,1,0:T(1,128)}, u32[]{:S(2)}, u32[]{:S(2)}) async-start(f32[32,1,1360]{2,1,0:T(1,128)} %reshape.195), calls=%async_computation.3 | async-start | bytes 360448 | tf_op jit(solution)/shard_map/all_to_all | solution.py:116
  209.2 18.4 %copy-start.5 = (f32[1920]{0:T(1024)S(1)}, f32[1920]{0:T(1024)}, u32[]{:S(2)}) copy-start(f32[1920]{0:T(1024)} %reshape.187) | copy-start | bytes 23044
  217.7 19.2 %all-to-all-start.3 = ((bf16[32,2,680]{2,1,0:T(2,128)(2,1)}), bf16[32,2,680]{2,1,0:T(2,128)(2,1)}, u32[]{:S(2)}, u32[]{:S(2)}) async-start(bf16[32,2,680]{2,1,0:T(2,128)(2,1)} %reshape.197), calls=%async_computation.4 | async-start | bytes 196608 | tf_op jit(solution)/shard_map/all_to_all | solution.py:120
Sparse Core Ops, SparseCore 0:
  76.1 107.4 reduce-scatter.1
